TPU v7x, 128 devices: a whole 4x4x4 slice. The times are simulated.
128 devices in a mesh: seq: 64 (over z, x, y_lo, core), chan: 2 (over y_hi).
Axes of the slice: x: 4, y: 4 (y_hi: 2, y_lo: 2; y = y_hi * 2 + y_lo), z: 4, core: 2. Of those that a mesh axis runs over, the one named last changes fastest.
Arguments:
- signal: bfloat16 [2, 32768, 128], P('chan', 'seq'), may hold values from -6 to 6
- cotangent: bfloat16 [2, 32768, 128], P('chan', 'seq'), may hold values from -6 to 6
- band_freq: int32 [16], replicated, may hold values from 1 to 8191
- w_embed: float32 [32, 64], replicated, may hold values from -2 to 2
- b_embed: float32 [64], replicated, may hold values from -3.140625 to 3.140625
- w_out: float32 [64, 128], P(None, 'chan'), may hold values from -0.75 to 0.75
- decay: float32 [128], P('chan'), may hold values from 0.25 to 16, as said below
Outputs:
- conv_out: bfloat16 [2, 32768, 128], P('chan', 'seq')
- d_signal: bfloat16 [2, 32768, 128], P('chan', 'seq')
- grad_embed: float32 [32, 64], replicated
- grad_bias: float32 [64], replicated
- grad_out: float32 [64, 128], P(None, 'chan')
Inputs may be any that keep to these rules, and one draw needn't show every extreme that they name: decay rates are positive.
All inputs are finite; a program needn't handle non-finite values.
Results may differ from a plain program's by a relative error of at most 0.007.
Values may be sent and summed in bfloat16 or wider, within the bound.
No kernel may reach another device: no remote copies, remote signals or barrier semaphores. Data moves between devices by JAX's collectives and lax.ppermute only.
A program may use at most 192 MiB of HBM per device.

v0:
```python
import math
import jax
import jax.numpy as jnp
from jax import lax
from jax.sharding import PartitionSpec as P

exact_mode = lax.Precision.HIGHEST


def mat_dot(lhs_mat, rhs_mat):
    return jnp.dot(lhs_mat, rhs_mat, preferred_element_type=jnp.float32, precision=exact_mode)


def band_phase(band_freq, places, seq_total):
    upper_part = places // 1024
    lower_part = places % 1024
    partial_turn = upper_part[:, None] * band_freq[None, :] % seq_total
    wrapped = (partial_turn * 1024 + lower_part[:, None] * band_freq[None, :]) % seq_total
    return wrapped.astype(jnp.float32) * (2.0 * math.pi / seq_total)


def filter_parts(places, band_freq, w_embed, b_embed, w_out, decay, seq_total):
    phases = band_phase(band_freq, places, seq_total)
    features = jnp.concatenate([jnp.cos(phases), jnp.sin(phases)], axis=1)
    preact = mat_dot(features, w_embed) + b_embed[None, :]
    hidden = jnp.sin(preact)
    fraction = places.astype(jnp.float32) / seq_total
    envelope = (
        jnp.exp(-decay[None, :] * fraction[:, None]) * jnp.sqrt((1.0 + decay) / seq_total)[None, :]
    )
    taps = mat_dot(hidden, w_out) * envelope
    return (features, preact, hidden, taps, envelope)


def angle_table(rows_idx, cols_idx, modulus):
    wrapped = rows_idx[:, None] * cols_idx[None, :] % modulus
    angles = wrapped.astype(jnp.float32) * (2.0 * math.pi / modulus)
    return (jnp.cos(angles), jnp.sin(angles))


def local(signal, cotangent, band_freq, w_embed, b_embed, w_out, decay):
    devices = lax.axis_size("seq")
    rank_seq = lax.axis_index("seq")
    seg_len = signal.shape[1] * 2
    channels = signal.shape[2] // 2
    block_w = seg_len // devices
    width = block_w * channels
    rows_all = 2 * devices
    pair = rows_all // devices
    seq_total = seg_len * devices
    fft_size = 2 * seq_total
    inv_scale = 1.0 / fft_size
    n_arr = 3
    dev_ids = jnp.arange(devices, dtype=jnp.int32)
    row_ids = jnp.arange(rows_all, dtype=jnp.int32)
    blk_ids = jnp.arange(block_w, dtype=jnp.int32)
    lane_blk = jnp.arange(width, dtype=jnp.int32) // channels
    b_lane = rank_seq * block_w + lane_blk
    src = jnp.stack([signal.reshape(devices, width), cotangent.reshape(devices, width)], axis=1)
    cols = lax.all_to_all(src, "seq", split_axis=0, concat_axis=0, tiled=True)
    places = (dev_ids[:, None] * seg_len + rank_seq * block_w + blk_ids[None, :]).reshape(-1)
    features, preact, hidden, taps, envelope = filter_parts(
        places, band_freq, w_embed, b_embed, w_out, decay, seq_total
    )
    stacked = jnp.concatenate(
        [cols.astype(jnp.float32), taps.reshape(devices, 1, width)], axis=1
    ).reshape(devices, n_arr * width)
    col_cos, col_sin = angle_table(row_ids, dev_ids, rows_all)
    y_re = mat_dot(col_cos, stacked).reshape(rows_all, n_arr, width)
    y_im = -mat_dot(col_sin, stacked).reshape(rows_all, n_arr, width)
    tw_cos, tw_sin = angle_table(row_ids, b_lane, fft_size)
    tw_cos = tw_cos[:, None, :]
    tw_sin = tw_sin[:, None, :]
    t_re = y_re * tw_cos + y_im * tw_sin
    t_im = y_im * tw_cos - y_re * tw_sin
    spec = jnp.stack([t_re, t_im], axis=1)
    spec = lax.all_to_all(spec, "seq", split_axis=0, concat_axis=0, tiled=True)
    q_cos, q_sin = angle_table(dev_ids, dev_ids, devices)
    stage_a = mat_dot(jnp.concatenate([q_cos, q_sin], axis=0), spec.reshape(devices, -1))
    stage_a = stage_a.reshape(2, devices, pair, 2, n_arr, width)
    a_re = stage_a[0, :, :, 0] + stage_a[1, :, :, 1]
    a_im = stage_a[0, :, :, 1] - stage_a[1, :, :, 0]
    mid_cos, mid_sin = angle_table(dev_ids, lane_blk, seg_len)
    mid_cos = mid_cos[:, None, None, :]
    mid_sin = mid_sin[:, None, None, :]
    b_re = (a_re * mid_cos + a_im * mid_sin).reshape(devices, pair, n_arr, block_w, channels)
    b_im = (a_im * mid_cos - a_re * mid_sin).reshape(devices, pair, n_arr, block_w, channels)
    m_cos, m_sin = angle_table(blk_ids, blk_ids, block_w)

    def blk_mix(table, vals):
        return jnp.einsum(
            "mb,qkzbc->qkzmc", table, vals, preferred_element_type=jnp.float32, precision=exact_mode
        )

    s_re = blk_mix(m_cos, b_re) + blk_mix(m_sin, b_im)
    s_im = blk_mix(m_cos, b_im) - blk_mix(m_sin, b_re)
    sig_r, cot_r, tap_r = (s_re[:, :, 0], s_re[:, :, 1], s_re[:, :, 2])
    sig_i, cot_i, tap_i = (s_im[:, :, 0], s_im[:, :, 1], s_im[:, :, 2])
    prod_r = jnp.stack(
        [
            sig_r * tap_r - sig_i * tap_i,
            cot_r * tap_r + cot_i * tap_i,
            cot_r * sig_r + cot_i * sig_i,
        ],
        axis=2,
    )
    prod_i = jnp.stack(
        [
            sig_r * tap_i + sig_i * tap_r,
            cot_i * tap_r - cot_r * tap_i,
            cot_i * sig_r - cot_r * sig_i,
        ],
        axis=2,
    )
    u_re = blk_mix(m_cos, prod_r) - blk_mix(m_sin, prod_i)
    u_im = blk_mix(m_cos, prod_i) + blk_mix(m_sin, prod_r)
    u_re = u_re.reshape(devices, pair, n_arr, width)
    u_im = u_im.reshape(devices, pair, n_arr, width)
    v_re = u_re * mid_cos - u_im * mid_sin
    v_im = u_im * mid_cos + u_re * mid_sin
    v_all = jnp.stack([v_re, v_im]).reshape(2 * devices, -1)
    inv_mat = jnp.concatenate(
        [jnp.concatenate([q_cos, -q_sin], axis=1), jnp.concatenate([q_sin, q_cos], axis=1)], axis=0
    )
    w_all = mat_dot(inv_mat, v_all).reshape(2, devices, pair, n_arr, width)
    b_rows = dev_ids[:, None] * block_w + lane_blk[None, :]
    k1_own = rank_seq * pair + jnp.arange(pair, dtype=jnp.int32)
    ex_ang = b_rows[:, None, :] * k1_own[None, :, None] % fft_size
    ex_ang = ex_ang.astype(jnp.float32) * (2.0 * math.pi / fft_size)
    ex_cos = jnp.cos(ex_ang)[:, :, None, :]
    ex_sin = jnp.sin(ex_ang)[:, :, None, :]
    x_re = w_all[0] * ex_cos - w_all[1] * ex_sin
    x_im = w_all[0] * ex_sin + w_all[1] * ex_cos
    back = jnp.stack([x_re, x_im], axis=1)
    back = lax.all_to_all(back, "seq", split_axis=0, concat_axis=0, tiled=True)
    back = back.reshape(devices, 2, pair, n_arr * width)
    back = jnp.transpose(back, (1, 0, 2, 3)).reshape(2 * rows_all, n_arr * width)
    out_mat = jnp.concatenate([col_cos.T, -col_sin.T], axis=1)
    res = (mat_dot(out_mat, back) * inv_scale).reshape(devices, n_arr, width)
    rows_out = lax.all_to_all(
        res[:, 0:2].astype(jnp.bfloat16), "seq", split_axis=0, concat_axis=0, tiled=True
    )
    conv_out = rows_out[:, 0].reshape(1, seg_len // 2, 2 * channels)
    d_signal = rows_out[:, 1].reshape(1, seg_len // 2, 2 * channels)
    d_taps = res[:, 2].reshape(devices * block_w, channels)
    d_raw = d_taps * envelope
    d_preact = mat_dot(d_raw, w_out.T) * jnp.cos(preact)
    out_part = mat_dot(hidden.T, d_raw)
    embed_part = mat_dot(features.T, d_preact)
    bias_part = jnp.sum(d_preact, axis=0)
    out_sum = lax.psum(out_part, "seq")
    embed_all, bias_all = lax.psum((embed_part, bias_part), ("seq", "chan"))
    norm_scale = 1.0 / math.sqrt(seq_total)
    return (conv_out, d_signal, embed_all * norm_scale, bias_all * norm_scale, out_sum * norm_scale)


def solution(mesh):
    return jax.shard_map(
        local,
        mesh=mesh,
        in_specs=(
            P("chan", "seq", None),
            P("chan", "seq", None),
            P(),
            P(),
            P(),
            P(None, "chan"),
            P("chan"),
        ),
        out_specs=(P("chan", "seq", None), P("chan", "seq", None), P(), P(), P(None, "chan")),
        check_vma=False,
    )
```

profile of v0, /device:TPU:0, one launch (start us, length us, event | category | flops | bytes accessed | tf_op | source)
XLA Modules:
  0.0 615.8 jit_solution(7838954913175535610)
XLA Ops:
  4.4 9.9 %all-to-all-start = ((bf16[64,2,1024]{2,1,0:T(2,128)(2,1)}), bf16[64,2,1024]{2,1,0:T(2,128)(2,1)S(1)}, u32[]{:S(2)}, u32[]{:S(2)}) async-start(bf16[64,2,1024]{2,1,0:T(2,128)(2,1)} %pad_maximum_fusion.14), calls=%async_computation | async-start | bytes 524288 | tf_op jit(solution)/shard_map/all_to_all | solution.py:60
  29.3 4.1 copy.76
  33.4 6.9 %all-to-all-start.1 = ((f32[128,2,3,1024]{3,1,2,0:T(2,128)}), f32[128,2,3,1024]{3,1,2,0:T(2,128)S(1)}, u32[]{:S(2)}, u32[]{:S(2)}) async-start(f32[128,2,3,1024]{3,1,2,0:T(2,128)} %copy.76), calls=%async_computation.1 | async-start | bytes 6291456 | tf_op jit(solution)/shard_map/all_to_all | solution.py:77
  47.2 9.5 %fusion.38 = (f32[64,2,1024]{2,1,0:T(2,128)}, f32[64,2,1024]{2,1,0:T(2,128)}) fusion(s32[2]{0:T(128)S(1)} %iota_add_fusion.1, s32[64,1024]{1,0:T(8,128)S(1)} %broadcast_add_fusion), kind=kLoop, calls=%fused_computation.88 | loop fusion | flops 1835008 | bytes 1310728 | tf_op jit(solution)/shard_map/cos | solution.py:130
  56.8 23.2 %all-to-all-done.1 = f32[128,2,3,1024]{3,1,2,0:T(2,128)S(1)} async-done(((f32[128,2,3,1024]{3,1,2,0:T(2,128)}), f32[128,2,3,1024]{3,1,2,0:T(2,128)S(1)}, u32[]{:S(2)}, u32[]{:S(2)}) %all-to-all-start.1) | async-done | bytes 3145760 | tf_op jit(solution)/shard_map/all_to_all | solution.py:77
  83.7 4.3 reshape.397
  91.8 9.4 %fusion = f32[2,64,2,2,3,1024]{5,1,4,3,2,0:T(8,128)S(1)} fusion(f32[2,64,64,1,1,1]{2,1,5,4,3,0:T(8,128)} %bitcast.98, f32[2,2,3,1024,64]{3,2,1,0,4:T(4,128)} %dot_general.72), kind=kOutput, calls=%fused_computation.6 | convolution fusion | flops 1207959552 | bytes 9469952 | tf_op jit(solution)/shard_map/dot_general | solution.py:11
  110.0 5.5 fusion.51
  132.9 4.7 subtract_bitcast_fusion
  137.6 4.9 reshape.411
  142.5 6.4 %add_bitcast_fusion = f32[64,2,3,16,64]{4,3,2,1,0:T(8,128)} fusion(f32[64,2,3,64,16]{3,4,2,1,0:T(8,128)S(1)} %fusion.3, f32[64,2,1,16,64]{4,3,2,1,0:T(8,128)} %copy-done.5, f32[64,2,1,16,64]{4,3,2,1,0:T(8,128)} %copy-done.6, f32[64,2,1,16,64]{4,3,2,1,0:T(8,128)} %copy-done.4), kind=kOutput, calls=%fused_computation.9 | convolution fusion | flops 76680704 | bytes 4718592 | tf_op jit(solution)/shard_map/mb,qkzbc->qkzmc/dot_general | solution.py:91
  148.9 4.6 reshape.412
  157.1 4.1 copy.85
  161.2 5.0 reshape.400
  174.9 3.9 squeeze.5
  182.9 4.7 copy.86
  187.5 6.6 %all-to-all-start.2 = ((f32[64,2,2,3,1024]{4,2,3,1,0:T(2,128)}), f32[64,2,2,3,1024]{4,2,3,1,0:T(2,128)S(1)}, u32[]{:S(2)}, u32[]{:S(2)}) async-start(f32[64,2,2,3,1024]{4,2,3,1,0:T(2,128)} %copy.86), calls=%async_computation.2 | async-start | bytes 6291456 | tf_op jit(solution)/shard_map/all_to_all | solution.py:135
  194.9 38.9 %all-to-all-done.2 = f32[64,2,2,3,1024]{4,2,3,1,0:T(2,128)S(1)} async-done(((f32[64,2,2,3,1024]{4,2,3,1,0:T(2,128)}), f32[64,2,2,3,1024]{4,2,3,1,0:T(2,128)S(1)}, u32[]{:S(2)}, u32[]{:S(2)}) %all-to-all-start.2) | async-done | bytes 3145760 | tf_op jit(solution)/shard_map/all_to_all | solution.py:135
  237.4 5.0 reshape.401
  242.3 4.1 copy.88
  246.4 3.9 reshape.402
  259.9 64.6 %all-reduce = (f32[32,64]{1,0:T(8,128)S(1)}, f32[64]{0:T(128)S(1)}) all-reduce(f32[32,64]{1,0:T(8,128)S(1)} %fusion.53, f32[64]{0:T(128)S(1)} %get-tuple-element.41), channel_id=1, replica_groups=mesh['seq'=64,'chan'=2] {'seq','chan'}, use_global_device_ids=true, to_apply=%region_0.1 | all-reduce | flops 2112 | bytes 16896 | tf_op jit(solution)/shard_map/psum | solution.py:152
  325.1 5.9 all-to-all-start.3
  331.5 280.7 %psum.23 = f32[64,64]{1,0:T(8,128)S(1)} all-reduce(f32[64,64]{1,0:T(8,128)S(1)} %fusion.40), channel_id=1, replica_groups=mesh['seq'=64,'chan'=2] {'seq'}, use_global_device_ids=true, to_apply=%region_3.4 | all-reduce | flops 4096 | bytes 32768 | tf_op jit(solution)/shard_map/psum | solution.py:151
  (101 shorter events, 93.5 us)
Async XLA Ops:
  0.6 18.3 %copy-start = (f32[64,64]{1,0:T(8,128)S(1)}, f32[64,64]{1,0:T(8,128)}, u32[]{:S(2)}) copy-start(f32[64,64]{1,0:T(8,128)} %param.12) | copy-start | bytes 49156
  4.4 19.8 %all-to-all-start = ((bf16[64,2,1024]{2,1,0:T(2,128)(2,1)}), bf16[64,2,1024]{2,1,0:T(2,128)(2,1)S(1)}, u32[]{:S(2)}, u32[]{:S(2)}) async-start(bf16[64,2,1024]{2,1,0:T(2,128)(2,1)} %pad_maximum_fusion.14), calls=%async_computation | async-start | bytes 524288 | tf_op jit(solution)/shard_map/all_to_all | solution.py:60
  16.2 2.7 copy-start.13
  33.4 46.6 %all-to-all-start.1 = ((f32[128,2,3,1024]{3,1,2,0:T(2,128)}), f32[128,2,3,1024]{3,1,2,0:T(2,128)S(1)}, u32[]{:S(2)}, u32[]{:S(2)}) async-start(f32[128,2,3,1024]{3,1,2,0:T(2,128)} %copy.76), calls=%async_computation.1 | async-start | bytes 6291456 | tf_op jit(solution)/shard_map/all_to_all | solution.py:77
  41.2 0.6 copy-start.15
  109.9 5.5 copy-start.1
  110.0 5.5 copy-start.2
  110.0 5.5 copy-start.3
  126.2 6.8 %copy-start.6 = (f32[64,2,1,16,64]{4,3,2,1,0:T(8,128)}, f32[64,2,1,16,64]{4,3,2,1,0:T(8,128)S(1)}, u32[]{:S(2)}) copy-start(f32[64,2,1,16,64]{4,3,2,1,0:T(8,128)S(1)} %get-tuple-element.13) | copy-start | bytes 1572868
  126.9 6.0 copy-start.4
  126.9 6.0 copy-start.5
  148.9 4.6 copy-start.7
  148.9 4.6 copy-start.10
  148.9 4.6 copy-start.11
  171.9 7.0 %copy-start.8 = (f32[64,2,1024]{2,1,0:T(2,128)S(1)}, f32[64,2,1024]{2,1,0:T(2,128)}, u32[]{:S(2)}) copy-start(f32[64,2,1024]{2,1,0:T(2,128)} %get-tuple-element.25) | copy-start | bytes 1572868
  171.9 7.0 %copy-start.9 = (f32[64,2,1024]{2,1,0:T(2,128)S(1)}, f32[64,2,1024]{2,1,0:T(2,128)}, u32[]{:S(2)}) copy-start(f32[64,2,1024]{2,1,0:T(2,128)} %get-tuple-element.26) | copy-start | bytes 1572868
  187.5 46.3 %all-to-all-start.2 = ((f32[64,2,2,3,1024]{4,2,3,1,0:T(2,128)}), f32[64,2,2,3,1024]{4,2,3,1,0:T(2,128)S(1)}, u32[]{:S(2)}, u32[]{:S(2)}) async-start(f32[64,2,2,3,1024]{4,2,3,1,0:T(2,128)} %copy.86), calls=%async_computation.2 | async-start | bytes 6291456 | tf_op jit(solution)/shard_map/all_to_all | solution.py:135
  254.0 4.2 copy-start.12
  254.0 5.6 copy-start.14
  325.1 287.8 %all-to-all-start.3 = ((bf16[64,2,1024]{2,1,0:T(2,128)(2,1)}), bf16[64,2,1024]{2,1,0:T(2,128)(2,1)S(1)}, u32[]{:S(2)}, u32[]{:S(2)}) async-start(bf16[64,2,1024]{2,1,0:T(2,128)(2,1)} %slice.117), calls=%async_computation.3 | async-start | bytes 524288 | tf_op jit(solution)/shard_map/all_to_all | solution.py:140
where the time goes:
time: 627 us; the launch traced here: 616 us
  blocking collectives  345 us (55%)
  local copies, waits for them, and re-layouts  80.4 us (13%)
  waiting for transfers between devices  64.5 us (10%)
  matrix products  58.9 us (9%)
  other arithmetic  35.8 us (6%)
  starting transfers between devices  29.3 us (5%)
    psum x1, blocking collectives, local(): out_sum = lax.psum(out_part, 'seq')  281 us
    psum x1, blocking collectives, local(): embed_all, bias_all = lax.psum((embed_part, bias_part), ('seq', 'chan'))  64.6 us
    all_to_all x1, waiting for transfers between devices, local(): back = lax.all_to_all(back, 'seq', split_axis=0, concat_axis=0, tiled=True)  38.9 us
    dot_general x8, matrix products, blk_mix(): jnp.einsum('mb,qkzbc->qkzmc', table, vals, preferred_element_type=jnp.flo...  32.6 us
    dot_general x10, matrix products, mat_dot(): jnp.dot(lhs_mat, rhs_mat, preferred_element_type=jnp.float32, precision=e...  26.2 us
    all_to_all x1, waiting for transfers between devices, local(): spec = lax.all_to_all(spec, 'seq', split_axis=0, concat_axis=0, tiled=True)  23.2 us
  transfers between devices with their start and end apart: 4, of which 3 were waited for; matrix products, arithmetic and copies ran while one was open for 4% of the time, Pallas kernels for 0%

commit v1 on v0

--- a/solution.py
+++ b/solution.py
@@ -5,6 +5,11 @@
 from jax.sharding import PartitionSpec as P
 
 exact_mode = lax.Precision.HIGHEST
+
+
+def by_each_axis(x, inner_axis, outer_axis):
+    partial = lax.psum(x, inner_axis)
+    return lax.psum(partial, outer_axis)
 
 
 def mat_dot(lhs_mat, rhs_mat):
@@ -149,7 +154,7 @@
     embed_part = mat_dot(features.T, d_preact)
     bias_part = jnp.sum(d_preact, axis=0)
     out_sum = lax.psum(out_part, "seq")
-    embed_all, bias_all = lax.psum((embed_part, bias_part), ("seq", "chan"))
+    embed_all, bias_all = by_each_axis((embed_part, bias_part), "seq", "chan")
     norm_scale = 1.0 / math.sqrt(seq_total)
     return (conv_out, d_signal, embed_all * norm_scale, bias_all * norm_scale, out_sum * norm_scale)
 

time: 627 us -> 578 us (0.922)
  the two profiles are of different devices: /device:TPU:0 before, /device:TPU:1 now
where the time goes in v1:
time: 578 us; the launch traced here: 567 us
  blocking collectives  280 us (48%)
  local copies, waits for them, and re-layouts  80.5 us (14%)
  waiting for transfers between devices  73.5 us (13%)
  matrix products  58.9 us (10%)
  starting transfers between devices  36.7 us (6%)
  other arithmetic  35.8 us (6%)
    psum x1, blocking collectives, by_each_axis(): partial = lax.psum(x, inner_axis)  270 us
    all_to_all x1, waiting for transfers between devices, local(): back = lax.all_to_all(back, 'seq', split_axis=0, concat_axis=0, tiled=True)  39.3 us
    dot_general x8, matrix products, blk_mix(): jnp.einsum('mb,qkzbc->qkzmc', table, vals, preferred_element_type=jnp.flo...  32.7 us
    dot_general x10, matrix products, mat_dot(): jnp.dot(lhs_mat, rhs_mat, preferred_element_type=jnp.float32, precision=e...  26.2 us
    all_to_all x1, waiting for transfers between devices, local(): spec = lax.all_to_all(spec, 'seq', split_axis=0, concat_axis=0, tiled=True)  23.7 us
    all_to_all x1, starting transfers between devices, local(): lax.all_to_all(res[:, 0:2].astype(jnp.bfloat16), 'seq', split_axis=0, con...  12.3 us
  transfers between devices with their start and end apart: 4, of which 4 were waited for; matrix products, arithmetic and copies ran while one was open for 4% of the time, Pallas kernels for 0%

profile of v1, /device:TPU:1, one launch (start us, length us, event | category | flops | bytes accessed | tf_op | source)
XLA Modules:
  0.0 566.8 jit_solution(1130801036788273230)
XLA Ops:
  4.4 10.8 %all-to-all-start = ((bf16[64,2,1024]{2,1,0:T(2,128)(2,1)}), bf16[64,2,1024]{2,1,0:T(2,128)(2,1)S(1)}, u32[]{:S(2)}, u32[]{:S(2)}) async-start(bf16[64,2,1024]{2,1,0:T(2,128)(2,1)} %pad_maximum_fusion.14), calls=%async_computation | async-start | bytes 524288 | tf_op jit(solution)/shard_map/all_to_all | solution.py:65
  29.9 4.1 copy.76
  34.0 7.2 %all-to-all-start.1 = ((f32[128,2,3,1024]{3,1,2,0:T(2,128)}), f32[128,2,3,1024]{3,1,2,0:T(2,128)S(1)}, u32[]{:S(2)}, u32[]{:S(2)}) async-start(f32[128,2,3,1024]{3,1,2,0:T(2,128)} %copy.76), calls=%async_computation.1 | async-start | bytes 6291456 | tf_op jit(solution)/shard_map/all_to_all | solution.py:82
  48.2 9.5 %fusion.38 = (f32[64,2,1024]{2,1,0:T(2,128)}, f32[64,2,1024]{2,1,0:T(2,128)}) fusion(s32[2]{0:T(128)S(1)} %iota_add_fusion.1, s32[64,1024]{1,0:T(8,128)S(1)} %broadcast_add_fusion), kind=kLoop, calls=%fused_computation.88 | loop fusion | flops 1835008 | bytes 1310728 | tf_op jit(solution)/shard_map/cos | solution.py:135
  57.7 23.7 %all-to-all-done.1 = f32[128,2,3,1024]{3,1,2,0:T(2,128)S(1)} async-done(((f32[128,2,3,1024]{3,1,2,0:T(2,128)}), f32[128,2,3,1024]{3,1,2,0:T(2,128)S(1)}, u32[]{:S(2)}, u32[]{:S(2)}) %all-to-all-start.1) | async-done | bytes 3145760 | tf_op jit(solution)/shard_map/all_to_all | solution.py:82
  85.1 4.3 reshape.397
  93.2 9.4 %fusion = f32[2,64,2,2,3,1024]{5,1,4,3,2,0:T(8,128)S(1)} fusion(f32[2,64,64,1,1,1]{2,1,5,4,3,0:T(8,128)} %bitcast.98, f32[2,2,3,1024,64]{3,2,1,0,4:T(4,128)} %dot_general.72), kind=kOutput, calls=%fused_computation.6 | convolution fusion | flops 1207959552 | bytes 9469952 | tf_op jit(solution)/shard_map/dot_general | solution.py:16
  111.4 5.5 fusion.51
  134.4 4.7 subtract_bitcast_fusion
  139.0 4.9 reshape.411
  143.9 6.4 %add_bitcast_fusion = f32[64,2,3,16,64]{4,3,2,1,0:T(8,128)} fusion(f32[64,2,3,64,16]{3,4,2,1,0:T(8,128)S(1)} %fusion.3, f32[64,2,1,16,64]{4,3,2,1,0:T(8,128)} %copy-done.5, f32[64,2,1,16,64]{4,3,2,1,0:T(8,128)} %copy-done.6, f32[64,2,1,16,64]{4,3,2,1,0:T(8,128)} %copy-done.4), kind=kOutput, calls=%fused_computation.9 | convolution fusion | flops 76680704 | bytes 4718592 | tf_op jit(solution)/shard_map/mb,qkzbc->qkzmc/dot_general | solution.py:96
  150.3 4.6 reshape.412
  158.6 4.1 copy.85
  162.7 5.0 reshape.400
  176.4 3.9 squeeze.5
  184.3 4.7 copy.86
  188.9 6.3 %all-to-all-start.2 = ((f32[64,2,2,3,1024]{4,2,3,1,0:T(2,128)}), f32[64,2,2,3,1024]{4,2,3,1,0:T(2,128)S(1)}, u32[]{:S(2)}, u32[]{:S(2)}) async-start(f32[64,2,2,3,1024]{4,2,3,1,0:T(2,128)} %copy.86), calls=%async_computation.2 | async-start | bytes 6291456 | tf_op jit(solution)/shard_map/all_to_all | solution.py:140
  196.0 39.3 %all-to-all-done.2 = f32[64,2,2,3,1024]{4,2,3,1,0:T(2,128)S(1)} async-done(((f32[64,2,2,3,1024]{4,2,3,1,0:T(2,128)}), f32[64,2,2,3,1024]{4,2,3,1,0:T(2,128)S(1)}, u32[]{:S(2)}, u32[]{:S(2)}) %all-to-all-start.2) | async-done | bytes 3145760 | tf_op jit(solution)/shard_map/all_to_all | solution.py:140
  238.9 5.0 reshape.401
  243.8 4.1 copy.88
  261.4 270.4 %all-reduce = (f32[32,64]{1,0:T(8,128)S(1)}, f32[64]{0:T(128)S(1)}, f32[64,64]{1,0:T(8,128)S(1)}) all-reduce(f32[32,64]{1,0:T(8,128)S(1)} %fusion.53, f32[64]{0:T(128)S(1)} %get-tuple-element.44, f32[64,64]{1,0:T(8,128)S(1)} %fusion.40), channel_id=1, replica_groups=mesh['seq'=64,'chan'=2] {'seq'}, use_global_device_ids=true, to_apply=%region_0.1 | all-reduce | flops 6208 | bytes 49664 | tf_op jit(solution)/shard_map/psum | solution.py:11
  531.8 9.4 %all-reduce.1 = (f32[32,64]{1,0:T(8,128)S(1)}, f32[64]{0:T(128)S(1)}) all-reduce(f32[32,64]{1,0:T(8,128)S(1)} %get-tuple-element.7, f32[64]{0:T(128)S(1)} %get-tuple-element.8), channel_id=1, replica_groups=mesh['seq'=64,'chan'=2] {'chan'}, use_global_device_ids=true, to_apply=%region_1.2 | all-reduce | flops 2112 | bytes 16896 | tf_op jit(solution)/shard_map/psum | solution.py:12
  541.9 12.3 %all-to-all-start.3 = ((bf16[64,2,1024]{2,1,0:T(2,128)(2,1)}), bf16[64,2,1024]{2,1,0:T(2,128)(2,1)S(1)}, u32[]{:S(2)}, u32[]{:S(2)}) async-start(bf16[64,2,1024]{2,1,0:T(2,128)(2,1)} %slice.117), calls=%async_computation.3 | async-start | bytes 524288 | tf_op jit(solution)/shard_map/all_to_all | solution.py:145
  555.3 8.6 %all-to-all-done.3 = bf16[64,2,1024]{2,1,0:T(2,128)(2,1)S(1)} async-done(((bf16[64,2,1024]{2,1,0:T(2,128)(2,1)}), bf16[64,2,1024]{2,1,0:T(2,128)(2,1)S(1)}, u32[]{:S(2)}, u32[]{:S(2)}) %all-to-all-start.3) | async-done | bytes 262176 | tf_op jit(solution)/shard_map/all_to_all | solution.py:145
  (101 shorter events, 97.1 us)
Async XLA Ops:
  0.6 19.2 %copy-start = (f32[64,64]{1,0:T(8,128)S(1)}, f32[64,64]{1,0:T(8,128)}, u32[]{:S(2)}) copy-start(f32[64,64]{1,0:T(8,128)} %param.12) | copy-start | bytes 49156
  4.4 20.4 %all-to-all-start = ((bf16[64,2,1024]{2,1,0:T(2,128)(2,1)}), bf16[64,2,1024]{2,1,0:T(2,128)(2,1)S(1)}, u32[]{:S(2)}, u32[]{:S(2)}) async-start(bf16[64,2,1024]{2,1,0:T(2,128)(2,1)} %pad_maximum_fusion.14), calls=%async_computation | async-start | bytes 524288 | tf_op jit(solution)/shard_map/all_to_all | solution.py:65
  17.2 2.7 copy-start.13
  34.0 47.4 %all-to-all-start.1 = ((f32[128,2,3,1024]{3,1,2,0:T(2,128)}), f32[128,2,3,1024]{3,1,2,0:T(2,128)S(1)}, u32[]{:S(2)}, u32[]{:S(2)}) async-start(f32[128,2,3,1024]{3,1,2,0:T(2,128)} %copy.76), calls=%async_computation.1 | async-start | bytes 6291456 | tf_op jit(solution)/shard_map/all_to_all | solution.py:82
  42.2 0.6 copy-start.15
  111.4 5.5 copy-start.1
  111.4 5.5 copy-start.2
  111.4 5.5 copy-start.3
  127.6 6.8 %copy-start.6 = (f32[64,2,1,16,64]{4,3,2,1,0:T(8,128)}, f32[64,2,1,16,64]{4,3,2,1,0:T(8,128)S(1)}, u32[]{:S(2)}) copy-start(f32[64,2,1,16,64]{4,3,2,1,0:T(8,128)S(1)} %get-tuple-element.16) | copy-start | bytes 1572868
  128.3 6.0 %copy-start.4 = (f32[64,2,1,16,64]{4,3,2,1,0:T(8,128)}, f32[64,2,1,16,64]{4,3,2,1,0:T(8,128)S(1)}, u32[]{:S(2)}) copy-start(f32[64,2,1,16,64]{4,3,2,1,0:T(8,128)S(1)} %get-tuple-element.12) | copy-start | bytes 1572868
  128.3 6.0 %copy-start.5 = (f32[64,2,1,16,64]{4,3,2,1,0:T(8,128)}, f32[64,2,1,16,64]{4,3,2,1,0:T(8,128)S(1)}, u32[]{:S(2)}) copy-start(f32[64,2,1,16,64]{4,3,2,1,0:T(8,128)S(1)} %get-tuple-element.13) | copy-start | bytes 1572868
  150.3 4.6 copy-start.7
  150.3 4.6 copy-start.10
  150.3 4.6 copy-start.11
  173.3 7.0 %copy-start.8 = (f32[64,2,1024]{2,1,0:T(2,128)S(1)}, f32[64,2,1024]{2,1,0:T(2,128)}, u32[]{:S(2)}) copy-start(f32[64,2,1024]{2,1,0:T(2,128)} %get-tuple-element.28) | copy-start | bytes 1572868
  173.3 7.0 %copy-start.9 = (f32[64,2,1024]{2,1,0:T(2,128)S(1)}, f32[64,2,1024]{2,1,0:T(2,128)}, u32[]{:S(2)}) copy-start(f32[64,2,1024]{2,1,0:T(2,128)} %get-tuple-element.29) | copy-start | bytes 1572868
  188.9 46.3 %all-to-all-start.2 = ((f32[64,2,2,3,1024]{4,2,3,1,0:T(2,128)}), f32[64,2,2,3,1024]{4,2,3,1,0:T(2,128)S(1)}, u32[]{:S(2)}, u32[]{:S(2)}) async-start(f32[64,2,2,3,1024]{4,2,3,1,0:T(2,128)} %copy.86), calls=%async_computation.2 | async-start | bytes 6291456 | tf_op jit(solution)/shard_map/all_to_all | solution.py:140
  255.4 4.2 copy-start.12
  255.4 5.6 copy-start.14
  541.9 22.0 %all-to-all-start.3 = ((bf16[64,2,1024]{2,1,0:T(2,128)(2,1)}), bf16[64,2,1024]{2,1,0:T(2,128)(2,1)S(1)}, u32[]{:S(2)}, u32[]{:S(2)}) async-start(bf16[64,2,1024]{2,1,0:T(2,128)(2,1)} %slice.117), calls=%async_computation.3 | async-start | bytes 524288 | tf_op jit(solution)/shard_map/all_to_all | solution.py:145
